TPU v7x, 32 devices: a whole 2x2x4 slice. The times are simulated.
32 devices in a mesh: tm: 4 (over y, x), series: 8 (over z, core).
Axes of the slice: x: 2, y: 2, z: 4, core: 2. Of those that a mesh axis runs over, the one named last changes fastest.
Arguments:
- codes: int32 [8, 512], P(None, ('tm', 'series')), may hold values from 0 to 916478, as said below
- owner_slot: int32 [8], replicated, may hold values from 0 to 7, each once
- edges: int32 [4096], replicated, may hold values from 0 to 2096640, as said below
- w_in: bfloat16 [128, 2304], replicated, may hold values from -0.09375 to 0.09375
- w_dt: bfloat16 [128, 32], replicated, may hold values from -0.5 to 0.5
- dt_bias: float32 [32], replicated, may hold values from -1 to 1
- decay_rate: float32 [32], replicated, may hold values from 1e-05 to 0.1
- grad_out: bfloat16 [8, 512, 2048], P('series', 'tm'), may hold values from -6 to 6
Outputs:
- ssd_output: bfloat16 [8, 512, 2048], P('series', 'tm')
- grad_in: float32 [128, 2304], replicated
Inputs may be any that keep to these rules, and one draw needn't show every extreme that they name: `codes`: each row is one series in the order of ingestion slots. edges[0] is 0 and edges rise strictly.
All inputs are finite; a program needn't handle non-finite values.
Results may differ from a plain program's by a relative error of at most 0.0062.
The roundings to bfloat16 on the way count: a program that leaves them out, or rounds other values in their place, can miss the bound.
Values sent between devices are 32-bit elements; how exact they have to be, the bound alone decides.
No kernel may reach another device: no remote copies, remote signals or barrier semaphores. Data moves between devices by JAX's collectives and lax.ppermute only.
A program may use at most 128 MiB of HBM per device.

v0:
```python
import math
import jax
import jax.numpy as jnp
from jax import lax
from jax.sharding import PartitionSpec as P

code_ceiling = 2097152.0


def carried_in(array, axis, combine, identity, reverse):
    count, position = (lax.axis_size(axis), lax.axis_index(axis))
    everything = jax.tree.map(lambda part: lax.all_gather(part, axis), array)
    start = jax.tree.map(
        lambda part, zero: jnp.broadcast_to(jnp.asarray(zero, part.dtype), part.shape),
        array,
        identity,
    )

    def lap(k, before):
        at = count - 1 - k if reverse else k
        reached = at > position if reverse else at < position
        new = combine(before, jax.tree.map(lambda part: part[at], everything))
        return jax.tree.map(lambda a, b: jnp.where(reached, a, b), new, before)

    return lax.fori_loop(0, count, lap, start)


def decay_matrix(cum_decay):
    row_count = cum_decay.shape[0]
    causal = jnp.arange(row_count)[:, None] >= jnp.arange(row_count)[None, :]
    log_span = cum_decay.T[:, :, None] - cum_decay.T[:, None, :]
    return jnp.where(causal[None], jnp.exp(jnp.where(causal[None], log_span, -60.0)), 0.0)


def carry_combine(earlier, later):
    return (earlier[0] * later[0], later[0][:, None, None] * earlier[1] + later[1])


def on_device(codes, owner_slot, edges, w_in, w_dt, dt_bias, decay_rate, grad_out):
    fl = jnp.float32
    half = jnp.bfloat16
    tok_rows = grad_out.shape[1]
    head_count = dt_bias.shape[0]
    inner_width = grad_out.shape[2]
    head_dim = inner_width // head_count
    state_dim = (w_in.shape[1] - inner_width) // 2
    seq_len = tok_rows * lax.axis_size("tm")
    series_count = lax.axis_size("series")
    ordered = jnp.take(codes, owner_slot, axis=0).astype(fl)
    own_series = lax.all_to_all(ordered, "series", split_axis=0, concat_axis=1, tiled=True)
    reading = own_series[0]
    edge_float = edges.astype(fl)
    upper_edge = jnp.concatenate([edge_float[1:], jnp.full((1,), code_ceiling, fl)])
    onehot = (
        (edge_float[None, :] <= reading[:, None]) & (upper_edge[None, :] > reading[:, None])
    ).astype(fl)
    counts = lax.psum(jnp.sum(onehot, axis=0), "tm")
    before = jnp.cumsum(counts) - counts
    bin_table = jnp.stack([before, counts, edge_float, upper_edge - edge_float], axis=1)
    picked = jnp.dot(onehot, bin_table, precision=lax.Precision.HIGHEST)
    within_bin = (reading - picked[:, 2]) / picked[:, 3]
    quantile = (picked[:, 0] + picked[:, 1] * within_bin) / seq_len
    frequency = (jnp.arange(w_in.shape[0], dtype=fl) + 0.5) * math.pi
    features = jnp.cos(quantile[:, None] * frequency).astype(half)
    projected = jnp.dot(features, w_in, preferred_element_type=fl).astype(half)
    x_heads = projected[:, :inner_width].reshape(tok_rows, head_count, head_dim)
    b_proj = projected[:, inner_width : inner_width + state_dim]
    c_proj = projected[:, inner_width + state_dim :]
    step_size = jax.nn.softplus(dt_bias + jnp.dot(features, w_dt, preferred_element_type=fl))
    cum_decay = jnp.cumsum(-step_size * decay_rate, axis=0)
    tail_factor = jnp.exp(cum_decay[-1][None, :] - cum_decay) * step_size
    head_factor = jnp.exp(cum_decay)
    grad_heads = grad_out[0].reshape(tok_rows, head_count, head_dim)
    masked = decay_matrix(cum_decay) * step_size.T[:, None, :]
    scores = jnp.dot(c_proj, b_proj.T, preferred_element_type=fl)
    weights = (scores[None] * masked).astype(half)
    x_weighted = (x_heads * tail_factor[:, :, None]).astype(half)
    state_local = jnp.einsum("thp,tn->hpn", x_weighted, b_proj, preferred_element_type=fl)
    block_gate = jnp.exp(cum_decay[-1])
    grad_weighted = (grad_heads * head_factor[:, :, None]).astype(half)
    adjoint_local = jnp.einsum("thp,tn->hpn", grad_weighted, c_proj, preferred_element_type=fl)
    identity = (jnp.ones((head_count,), fl), jnp.zeros((head_count, head_dim, state_dim), fl))
    _, state_in = carried_in((block_gate, state_local), "tm", carry_combine, identity, False)
    _, adjoint_in = carried_in((block_gate, adjoint_local), "tm", carry_combine, identity, True)
    state_half = state_in.astype(half)
    adjoint_half = adjoint_in.astype(half)
    output = jnp.einsum("hts,shp->thp", weights, x_heads, preferred_element_type=fl)
    output = (
        output
        + jnp.einsum("tn,hpn->thp", c_proj, state_half, preferred_element_type=fl)
        * head_factor[:, :, None]
    )
    ssd_output = output.reshape(1, tok_rows, inner_width).astype(half)
    grad_x = jnp.einsum("hts,thp->shp", weights, grad_heads, preferred_element_type=fl)
    grad_x = (
        grad_x
        + jnp.einsum("sn,hpn->shp", b_proj, adjoint_half, preferred_element_type=fl)
        * tail_factor[:, :, None]
    )
    pair_scores = jnp.einsum("thp,shp->hts", grad_heads, x_heads, preferred_element_type=fl)
    pair_mixed = jnp.sum(pair_scores * masked, axis=0).astype(half)
    grad_b = jnp.dot(pair_mixed.T, c_proj, preferred_element_type=fl)
    grad_b = grad_b + jnp.einsum("shp,hpn->sn", x_weighted, adjoint_half, preferred_element_type=fl)
    grad_c = jnp.dot(pair_mixed, b_proj, preferred_element_type=fl)
    grad_c = grad_c + jnp.einsum(
        "thp,hpn->tn", grad_weighted, state_half, preferred_element_type=fl
    )
    grad_rows = jnp.concatenate(
        [
            grad_x.reshape(tok_rows, inner_width).astype(half),
            grad_b.astype(half),
            grad_c.astype(half),
        ],
        axis=1,
    )
    local_grad = jnp.einsum("tf,tw->fw", features, grad_rows, preferred_element_type=fl)
    share_grad = lax.psum_scatter(local_grad, "series", scatter_dimension=1, tiled=True)
    share_grad = lax.psum(share_grad, "tm")
    total_grad = lax.all_gather(share_grad, "series", axis=1, tiled=True)
    grad_in = total_grad / math.sqrt(series_count * seq_len)
    return (ssd_output, grad_in)


def solution(mesh):
    return jax.shard_map(
        on_device,
        mesh=mesh,
        in_specs=(P(None, ("tm", "series")), P(), P(), P(), P(), P(), P(), P("series", "tm", None)),
        out_specs=(P("series", "tm", None), P()),
        check_vma=False,
    )
```

profile of v0, /device:TPU:0, one launch (start us, length us, event | category | flops | bytes accessed | tf_op | source)
XLA Modules:
  0.0 267.1 jit_solution(18337310911339434361)
XLA Ops:
  10.5 6.3 %all-to-all-start = ((f32[8,1,16]{2,1,0:T(1,128)}), f32[8,1,16]{2,1,0:T(1,128)S(1)}, u32[]{:S(2)}, u32[]{:S(2)}) async-start(f32[8,1,16]{2,1,0:T(1,128)} %bitcast.1), calls=%async_computation | async-start | bytes 8192 | tf_op jit(solution)/shard_map/all_to_all | solution.py:50
  19.8 2.5 all-to-all-done
  24.0 16.0 %psum.14 = f32[4096]{0:T(1024)S(1)} all-reduce(f32[4096]{0:T(1024)S(1)} %convert_reduce_fusion), channel_id=1, replica_groups=mesh['tm'=4,'series'=8] {'tm'}, use_global_device_ids=true, to_apply=%region_1.2 | all-reduce | flops 4096 | bytes 32768 | tf_op jit(solution)/shard_map/psum | solution.py:57
  46.9 7.0 %all-gather.2 = f32[4,1,32]{2,1,0:T(1,128)S(1)} all-gather(f32[1,1,32]{2,1,0:T(1,128)S(1)} %get-tuple-element.295), channel_id=1, replica_groups=mesh['tm'=4,'series'=8] {'tm'}, dimensions={0}, use_global_device_ids=true | all-gather | bytes 640 | tf_op jit(solution)/shard_map/all_gather | solution.py:12
  54.8 2.6 fusion.2
  59.3 2.3 convolution_bitcast_fusion
  61.6 33.1 %all-gather.11.cloned.1.call-done = f32[128,64,128]{2,1,0:T(8,128)} async-done(((f32[32,64,128]{2,1,0:T(8,128)}), f32[128,64,128]{2,1,0:T(8,128)}) %all-gather.11.cloned.1.call-update) | async-done | bytes 4194320 | tf_op jit(solution)/shard_map/all_gather | solution.py:12
  94.7 6.0 %while.31 = (s32[]{:T(128)}, f32[32,64,128]{2,1,0:T(8,128)S(1)}, s32[]{:T(128)}, f32[4,32]{1,0:T(4,128)S(1)}, f32[4,32,64,128]{3,2,1,0:T(8,128)}, /*index=5*/s32[]{:T(128)}, s32[]{:T(128)}, s32[]{:T(128)}, s32[]{:T(128)}) while((s32[]{:T(128)}, f32[32,64,128]{2,1,0:T(8,128)S(1)}, s32[]{:T(128)}, f32[4,32]{1,0:T(4,128)S(1)}, ...), condition=%wide.region_8.9_spmd.clone, body=%wide.region_7.8_spmd.clone.sunk | while | flops 1048584 | bytes 3146279 | solution.py:25
  94.7 1.5 fusion.79
  96.2 1.5 fusion.79
  97.7 1.5 fusion.79
  99.3 1.5 fusion.79
  100.7 1.5 fusion.10
  102.3 1.9 fusion.7
  104.1 45.2 %all-gather.9.cloned.1.call-done = f32[128,64,128]{2,1,0:T(8,128)} async-done(((f32[32,64,128]{2,1,0:T(8,128)}), f32[128,64,128]{2,1,0:T(8,128)}) %all-gather.9.cloned.1.call-update) | async-done | bytes 4194320 | tf_op jit(solution)/shard_map/all_gather | solution.py:12
  149.3 6.0 %while.30 = (s32[]{:T(128)}, f32[32,64,128]{2,1,0:T(8,128)S(1)}, s32[]{:T(128)}, f32[4,32]{1,0:T(4,128)S(1)}, f32[4,32,64,128]{3,2,1,0:T(8,128)}, /*index=5*/s32[]{:T(128)}, s32[]{:T(128)}) while((s32[]{:T(128)}, f32[32,64,128]{2,1,0:T(8,128)S(1)}, s32[]{:T(128)}, f32[4,32]{1,0:T(4,128)S(1)}, f32[4,32,64,128]{3,2,1,0:T(8,128)}, ...), condition=%wide.region_6.7_spmd.clone, body=%wide.region_5.6_spmd.clone.sunk | while | flops 1048580 | bytes 3146217 | solution.py:25
  149.3 1.5 fusion.78
  150.9 1.5 fusion.78
  152.4 1.5 fusion.78
  153.9 1.5 fusion.78
  155.7 1.6 fusion.15
  157.4 32.7 %reduce-scatter.2.cloned.1.call-done = f32[128,288]{0,1:T(8,128)} async-done(((f32[128,2304]{0,1:T(8,128)}), f32[128,288]{0,1:T(8,128)}) %reduce-scatter.2.cloned.1.call-update) | async-done | bytes 147472 | tf_op jit(solution)/shard_map/reduce_scatter | solution.py:117
  190.1 43.2 %all-reduce.2.cloned.1.call-done = f32[128,288]{0,1:T(8,128)} async-done(((f32[128,288]{0,1:T(8,128)}), f32[128,288]{0,1:T(8,128)}) %all-reduce.2.cloned.1.call-update) | async-done | bytes 147472 | tf_op jit(solution)/shard_map/psum | solution.py:118
  236.8 21.0 %all-gather.7.cloned.1.call-done = f32[128,2304]{0,1:T(8,128)} async-done(((f32[128,288]{0,1:T(8,128)}), f32[128,2304]{0,1:T(8,128)}) %all-gather.7.cloned.1.call-update) | async-done | bytes 1179664 | tf_op jit(solution)/shard_map/all_gather | solution.py:119
  (85 shorter events, 24.1 us)
Async XLA Ops:
  7.2 34.8 %copy-start = (bf16[128,2304]{1,0:T(8,128)(2,1)S(1)}, bf16[128,2304]{1,0:T(8,128)(2,1)}, u32[]{:S(2)}) copy-start(bf16[128,2304]{1,0:T(8,128)(2,1)} %param.15) | copy-start | bytes 1769476
  10.5 11.8 %all-to-all-start = ((f32[8,1,16]{2,1,0:T(1,128)}), f32[8,1,16]{2,1,0:T(1,128)S(1)}, u32[]{:S(2)}, u32[]{:S(2)}) async-start(f32[8,1,16]{2,1,0:T(1,128)} %bitcast.1), calls=%async_computation | async-start | bytes 8192 | tf_op jit(solution)/shard_map/all_to_all | solution.py:50
  16.8 77.9 %all-gather.11.cloned.1.call-start = ((), (), s32[]{:S(2)}) async-start(), calls=%async_computation.6 | async-start | bytes 5242880 | tf_op jit(solution)/shard_map/all_gather | solution.py:12
  18.5 24.1 %copy-start.7 = (bf16[128,32]{0,1:T(8,128)(2,1)S(1)}, bf16[128,32]{0,1:T(8,128)(2,1)}, u32[]{:S(2)}) copy-start(bf16[128,32]{0,1:T(8,128)(2,1)} %param.16) | copy-start | bytes 24580
  18.5 24.1 %copy-start.8 = (f32[32]{0:T(128)S(1)}, f32[32]{0:T(128)}, u32[]{:S(2)}) copy-start(f32[32]{0:T(128)} %param.17) | copy-start | bytes 388
  18.5 24.6 %copy-start.6 = (f32[32]{0:T(128)S(1)}, f32[32]{0:T(128)}, u32[]{:S(2)}) copy-start(f32[32]{0:T(128)} %param.18) | copy-start | bytes 388
  42.6 2.7 %copy-start.3 = (bf16[128,2304]{1,0:T(8,128)(2,1)}, bf16[128,2304]{1,0:T(8,128)(2,1)S(1)}, u32[]{:S(2)}) copy-start(bf16[128,2304]{1,0:T(8,128)(2,1)S(1)} %convolution_convert_fusion) | copy-start | bytes 1769476
  44.8 104.5 %all-gather.9.cloned.1.call-start = ((), (), s32[]{:S(2)}) async-start(), calls=%async_computation.5 | async-start | bytes 5242880 | tf_op jit(solution)/shard_map/all_gather | solution.py:12
  45.2 1.5 copy-start.1
  46.7 143.3 %reduce-scatter.2.cloned.1.call-start = ((), (), s32[]{:S(2)}) async-start(), calls=%async_computation.2 | async-start | bytes 1327104 | tf_op jit(solution)/shard_map/reduce_scatter | solution.py:117
  100.7 1.5 copy-start.5
  149.3 6.4 %copy-start.4 = (bf16[128,32,64]{0,2,1:T(8,128)(2,1)S(1)}, bf16[128,32,64]{0,2,1:T(8,128)(2,1)}, u32[]{:S(2)}) copy-start(bf16[128,32,64]{0,2,1:T(8,128)(2,1)} %fusion.7) | copy-start | bytes 1572868
  155.3 78.0 %copy-start.2 = (bf16[128,2048]{0,1:T(8,128)(2,1)S(1)}, bf16[128,2048]{0,1:T(8,128)(2,1)}, u32[]{:S(2)}) copy-start(bf16[128,2048]{0,1:T(8,128)(2,1)} %copy-done.1) | copy-start | bytes 1572868
  157.3 76.0 %all-reduce.2.cloned.1.call-start = ((), (), s32[]{:S(2)}) async-start(), calls=%async_computation.3 | async-start | bytes 294912 | tf_op jit(solution)/shard_map/psum | solution.py:118
  190.1 67.7 %all-gather.7.cloned.1.call-start = ((), (), s32[]{:S(2)}) async-start(), calls=%async_computation.4 | async-start | bytes 1327104 | tf_op jit(solution)/shard_map/all_gather | solution.py:119
Sparse Core Ops, SparseCore 0:
  44.9 49.7 all-gather.10
  96.6 52.6 all-gather.8
  157.4 32.5 reduce-scatter.1
  192.8 40.4 all-reduce.1
  234.9 22.8 all-gather.6
where the time goes:
time: 268 us; the launch traced here: 267 us
  waiting for transfers between devices  178 us (66%)
  blocking collectives  23 us (9%)
  matrix products  20.3 us (8%)
  other arithmetic  18.5 us (7%)
  between operations  14.1 us (5%)
  local copies, waits for them, and re-layouts  6.62 us (2%)
  starting transfers between devices  6.53 us (2%)
    all_gather x2, waiting for transfers between devices, carried_in(): everything = jax.tree.map(lambda part: lax.all_gather(part, axis), array)  78.3 us
    psum x1, waiting for transfers between devices, on_device(): share_grad = lax.psum(share_grad, 'tm')  43.2 us
    reduce_scatter x1, waiting for transfers between devices, on_device(): lax.psum_scatter(local_grad, 'series', scatter_dimension=1, tiled=True)  32.7 us
    all_gather x1, waiting for transfers between devices, on_device(): total_grad = lax.all_gather(share_grad, 'series', axis=1, tiled=True)  21 us
    psum x1, blocking collectives, on_device(): counts = lax.psum(jnp.sum(onehot, axis=0), 'tm')  16 us
    select_n x8, other arithmetic, lap(): return jax.tree.map(lambda a, b: jnp.where(reached, a, b), new, before)  11.7 us
    all_gather x1, blocking collectives, carried_in(): everything = jax.tree.map(lambda part: lax.all_gather(part, axis), array)  6.99 us
    all_to_all x1, starting transfers between devices, on_device(): lax.all_to_all(ordered, 'series', split_axis=0, concat_axis=1, tiled=True)  6.33 us
  transfers between devices with their start and end apart: 6, of which 6 were waited for; matrix products, arithmetic and copies ran while one was open for 9% of the time, Pallas kernels for 0%

commit v1 on v0

--- a/solution.py
+++ b/solution.py
@@ -115,7 +115,7 @@
     )
     local_grad = jnp.einsum("tf,tw->fw", features, grad_rows, preferred_element_type=fl)
     share_grad = lax.psum_scatter(local_grad, "series", scatter_dimension=1, tiled=True)
-    share_grad = lax.psum(share_grad, "tm")
+    share_grad = jnp.sum(lax.all_gather(share_grad, "tm"), axis=0)
     total_grad = lax.all_gather(share_grad, "series", axis=1, tiled=True)
     grad_in = total_grad / math.sqrt(series_count * seq_len)
     return (ssd_output, grad_in)

time: 268 us -> 238 us (0.89)
  waiting for transfers between devices: 178 us -> 133 us
  blocking collectives: 23 us -> 36 us
    psum x1 -> x0, waiting for transfers between devices: 43.2 us -> none  [on_device(): share_grad = lax.psum(share_grad, 'tm')]
    all_gather x0 -> x1, blocking collectives: none -> 13 us  [on_device(): share_grad = jnp.sum(lax.all_gather(share_grad, 'tm'), axis=0)]
  transfers between devices with their start and end apart: 6 -> 5, of which waited for: 6 -> 5; matrix products, arithmetic and copies ran while one was open for 9% -> 11% of each run, Pallas kernels for 0% -> 0%
where the time goes in v1:
time: 238 us; the launch traced here: 236 us
  waiting for transfers between devices  133 us (56%)
  blocking collectives  36 us (15%)
  matrix products  20.3 us (9%)
  other arithmetic  19.6 us (8%)
  between operations  14 us (6%)
  local copies, waits for them, and re-layouts  6.82 us (3%)
  starting transfers between devices  6.49 us (3%)
    all_gather x2, waiting for transfers between devices, carried_in(): everything = jax.tree.map(lambda part: lax.all_gather(part, axis), array)  78.3 us
    reduce_scatter x1, waiting for transfers between devices, on_device(): lax.psum_scatter(local_grad, 'series', scatter_dimension=1, tiled=True)  32.8 us
    all_gather x1, waiting for transfers between devices, on_device(): total_grad = lax.all_gather(share_grad, 'series', axis=1, tiled=True)  19.3 us
    psum x1, blocking collectives, on_device(): counts = lax.psum(jnp.sum(onehot, axis=0), 'tm')  16 us
    all_gather x1, blocking collectives, on_device(): share_grad = jnp.sum(lax.all_gather(share_grad, 'tm'), axis=0)  13 us
    select_n x8, other arithmetic, lap(): return jax.tree.map(lambda a, b: jnp.where(reached, a, b), new, before)  11.7 us
    all_gather x1, blocking collectives, carried_in(): everything = jax.tree.map(lambda part: lax.all_gather(part, axis), array)  6.99 us
    all_to_all x1, starting transfers between devices, on_device(): lax.all_to_all(ordered, 'series', split_axis=0, concat_axis=1, tiled=True)  6.33 us
  transfers between devices with their start and end apart: 5, of which 5 were waited for; matrix products, arithmetic and copies ran while one was open for 11% of the time, Pallas kernels for 0%

profile of v1, /device:TPU:0, one launch (start us, length us, event | category | flops | bytes accessed | tf_op | source)
XLA Modules:
  0.0 236.4 jit_solution(3595886966155110359)
XLA Ops:
  10.5 6.3 %all-to-all-start = ((f32[8,1,16]{2,1,0:T(1,128)}), f32[8,1,16]{2,1,0:T(1,128)S(1)}, u32[]{:S(2)}, u32[]{:S(2)}) async-start(f32[8,1,16]{2,1,0:T(1,128)} %bitcast.1), calls=%async_computation | async-start | bytes 8192 | tf_op jit(solution)/shard_map/all_to_all | solution.py:50
  19.8 2.5 %all-to-all-done = f32[8,1,16]{2,1,0:T(1,128)S(1)} async-done(((f32[8,1,16]{2,1,0:T(1,128)}), f32[8,1,16]{2,1,0:T(1,128)S(1)}, u32[]{:S(2)}, u32[]{:S(2)}) %all-to-all-start) | async-done | bytes 544 | tf_op jit(solution)/shard_map/all_to_all | solution.py:50
  24.0 16.0 %psum.7 = f32[4096]{0:T(1024)S(1)} all-reduce(f32[4096]{0:T(1024)S(1)} %convert_reduce_fusion), channel_id=1, replica_groups=mesh['tm'=4,'series'=8] {'tm'}, use_global_device_ids=true, to_apply=%region_1.2 | all-reduce | flops 4096 | bytes 32768 | tf_op jit(solution)/shard_map/psum | solution.py:57
  46.9 7.0 %all-gather.3 = f32[4,1,32]{2,1,0:T(1,128)S(1)} all-gather(f32[1,1,32]{2,1,0:T(1,128)S(1)} %get-tuple-element.295), channel_id=1, replica_groups=mesh['tm'=4,'series'=8] {'tm'}, dimensions={0}, use_global_device_ids=true | all-gather | bytes 640 | tf_op jit(solution)/shard_map/all_gather | solution.py:12
  54.8 2.6 %fusion.2 = bf16[128,128]{0,1:T(8,128)(2,1)S(1)} fusion(bf16[128,32,64]{0,2,1:T(8,128)(2,1)} %bitcast.110, bf16[128,32,64]{0,2,1:T(8,128)(2,1)S(1)} %bitcast.106, f32[32,128]{1,0:T(8,128)S(1)} %get-tuple-element.298, f32[32,128]{1,0:T(8,128)S(1)} %copy.51, pred[128,128]{0,1:T(8,128)(4,1)S(1)} %iota_compare_fusion), kind=kOutput, calls=%fused_computation.9 | convolution fusion | flops 70238208 | bytes 1130496 | tf_op jit(solution)/shard_map/thp,shp->hts/dot_general | solution.py:100
  59.3 2.4 convolution_bitcast_fusion
  61.6 33.1 %all-gather.12.cloned.1.call-done = f32[128,64,128]{2,1,0:T(8,128)} async-done(((f32[32,64,128]{2,1,0:T(8,128)}), f32[128,64,128]{2,1,0:T(8,128)}) %all-gather.12.cloned.1.call-update) | async-done | bytes 4194320 | tf_op jit(solution)/shard_map/all_gather | solution.py:12
  94.7 6.0 %while.31 = (s32[]{:T(128)}, f32[32,64,128]{2,1,0:T(8,128)S(1)}, s32[]{:T(128)}, f32[4,32]{1,0:T(4,128)S(1)}, f32[4,32,64,128]{3,2,1,0:T(8,128)}, /*index=5*/s32[]{:T(128)}, s32[]{:T(128)}, s32[]{:T(128)}, s32[]{:T(128)}) while((s32[]{:T(128)}, f32[32,64,128]{2,1,0:T(8,128)S(1)}, s32[]{:T(128)}, f32[4,32]{1,0:T(4,128)S(1)}, ...), condition=%wide.region_8.9_spmd.clone, body=%wide.region_7.8_spmd.clone.sunk | while | flops 1048584 | bytes 3146279 | solution.py:25
  94.7 1.5 fusion.79
  96.2 1.5 fusion.79
  97.8 1.5 fusion.79
  99.3 1.5 fusion.79
  100.8 1.5 fusion.10
  102.3 1.9 fusion.7
  104.1 45.2 %all-gather.10.cloned.1.call-done = f32[128,64,128]{2,1,0:T(8,128)} async-done(((f32[32,64,128]{2,1,0:T(8,128)}), f32[128,64,128]{2,1,0:T(8,128)}) %all-gather.10.cloned.1.call-update) | async-done | bytes 4194320 | tf_op jit(solution)/shard_map/all_gather | solution.py:12
  149.3 6.0 %while.30 = (s32[]{:T(128)}, f32[32,64,128]{2,1,0:T(8,128)S(1)}, s32[]{:T(128)}, f32[4,32]{1,0:T(4,128)S(1)}, f32[4,32,64,128]{3,2,1,0:T(8,128)}, /*index=5*/s32[]{:T(128)}, s32[]{:T(128)}) while((s32[]{:T(128)}, f32[32,64,128]{2,1,0:T(8,128)S(1)}, s32[]{:T(128)}, f32[4,32]{1,0:T(4,128)S(1)}, f32[4,32,64,128]{3,2,1,0:T(8,128)}, ...), condition=%wide.region_6.7_spmd.clone, body=%wide.region_5.6_spmd.clone.sunk | while | flops 1048580 | bytes 3146217 | solution.py:25
  149.3 1.5 fusion.78
  150.9 1.5 fusion.78
  152.4 1.5 fusion.78
  153.9 1.5 fusion.78
  155.7 1.6 fusion.15
  157.4 32.8 %reduce-scatter.2.cloned.1.call-done = f32[128,288]{0,1:T(8,128)} async-done(((f32[128,2304]{0,1:T(8,128)}), f32[128,288]{0,1:T(8,128)}) %reduce-scatter.2.cloned.1.call-update) | async-done | bytes 147472 | tf_op jit(solution)/shard_map/reduce_scatter | solution.py:117
  190.2 13.0 %all-gather.2 = f32[512,288]{0,1:T(8,128)S(1)} all-gather(f32[128,288]{0,1:T(8,128)} %reduce-scatter.2.cloned.1.call-done), channel_id=4, replica_groups=mesh['tm'=4,'series'=8] {'tm'}, dimensions={0}, use_global_device_ids=true | all-gather | bytes 737280 | tf_op jit(solution)/shard_map/all_gather | solution.py:118
  207.8 19.3 %all-gather.8.cloned.1.call-done = f32[128,2304]{0,1:T(8,128)} async-done(((f32[128,288]{0,1:T(8,128)}), f32[128,2304]{0,1:T(8,128)}) %all-gather.8.cloned.1.call-update) | async-done | bytes 1179664 | tf_op jit(solution)/shard_map/all_gather | solution.py:119
  (85 shorter events, 25.3 us)
Async XLA Ops:
  7.2 34.8 %copy-start = (bf16[128,2304]{1,0:T(8,128)(2,1)S(1)}, bf16[128,2304]{1,0:T(8,128)(2,1)}, u32[]{:S(2)}) copy-start(bf16[128,2304]{1,0:T(8,128)(2,1)} %param.15) | copy-start | bytes 1769476
  10.5 11.8 %all-to-all-start = ((f32[8,1,16]{2,1,0:T(1,128)}), f32[8,1,16]{2,1,0:T(1,128)S(1)}, u32[]{:S(2)}, u32[]{:S(2)}) async-start(f32[8,1,16]{2,1,0:T(1,128)} %bitcast.1), calls=%async_computation | async-start | bytes 8192 | tf_op jit(solution)/shard_map/all_to_all | solution.py:50
  16.8 77.9 %all-gather.12.cloned.1.call-start = ((), (), s32[]{:S(2)}) async-start(), calls=%async_computation.5 | async-start | bytes 5242880 | tf_op jit(solution)/shard_map/all_gather | solution.py:12
  18.5 24.1 %copy-start.7 = (bf16[128,32]{0,1:T(8,128)(2,1)S(1)}, bf16[128,32]{0,1:T(8,128)(2,1)}, u32[]{:S(2)}) copy-start(bf16[128,32]{0,1:T(8,128)(2,1)} %param.16) | copy-start | bytes 24580
  18.5 24.1 %copy-start.8 = (f32[32]{0:T(128)S(1)}, f32[32]{0:T(128)}, u32[]{:S(2)}) copy-start(f32[32]{0:T(128)} %param.17) | copy-start | bytes 388
  18.5 24.6 %copy-start.6 = (f32[32]{0:T(128)S(1)}, f32[32]{0:T(128)}, u32[]{:S(2)}) copy-start(f32[32]{0:T(128)} %param.18) | copy-start | bytes 388
  42.6 2.7 %copy-start.3 = (bf16[128,2304]{1,0:T(8,128)(2,1)}, bf16[128,2304]{1,0:T(8,128)(2,1)S(1)}, u32[]{:S(2)}) copy-start(bf16[128,2304]{1,0:T(8,128)(2,1)S(1)} %convolution_convert_fusion) | copy-start | bytes 1769476
  44.8 104.5 %all-gather.10.cloned.1.call-start = ((), (), s32[]{:S(2)}) async-start(), calls=%async_computation.4 | async-start | bytes 5242880 | tf_op jit(solution)/shard_map/all_gather | solution.py:12
  45.2 1.6 copy-start.1
  46.7 143.5 %reduce-scatter.2.cloned.1.call-start = ((), (), s32[]{:S(2)}) async-start(), calls=%async_computation.2 | async-start | bytes 1327104 | tf_op jit(solution)/shard_map/reduce_scatter | solution.py:117
  100.7 1.5 copy-start.5
  149.3 6.4 %copy-start.4 = (bf16[128,32,64]{0,2,1:T(8,128)(2,1)S(1)}, bf16[128,32,64]{0,2,1:T(8,128)(2,1)}, u32[]{:S(2)}) copy-start(bf16[128,32,64]{0,2,1:T(8,128)(2,1)} %fusion.7) | copy-start | bytes 1572868
  157.3 47.1 %copy-start.2 = (bf16[128,2048]{0,1:T(8,128)(2,1)S(1)}, bf16[128,2048]{0,1:T(8,128)(2,1)}, u32[]{:S(2)}) copy-start(bf16[128,2048]{0,1:T(8,128)(2,1)} %copy-done.1) | copy-start | bytes 1572868
  157.3 69.8 %all-gather.8.cloned.1.call-start = ((), (), s32[]{:S(2)}) async-start(), calls=%async_computation.3 | async-start | bytes 1327104 | tf_op jit(solution)/shard_map/all_gather | solution.py:119
Sparse Core Ops, SparseCore 0:
  44.9 49.7 all-gather.11
  96.6 52.6 all-gather.9
  157.4 32.7 reduce-scatter.1
  204.6 22.5 all-gather.7
